TPU v7x, 32 devices: a whole 2x2x4 slice. The times are simulated.
32 devices in a mesh: groups: 2 (over y), ctx: 4 (over z), fsdp: 2 (over x), sub: 2 (over core).
Axes of the slice: x: 2, y: 2, z: 4, core: 2. Of those that a mesh axis runs over, the one named last changes fastest.
Arguments:
- layer_input: bfloat16 [4, 2048, 2304], P(('groups', 'fsdp'), ('ctx', 'sub')), parts along dimension 0, may hold values from -6 to 6
- query_heads: bfloat16 [4, 2048, 1024], P(('groups', 'fsdp'), ('ctx', 'sub')), parts along dimension 0, may hold values from -11 to 11
- key_heads: bfloat16 [4, 2048, 512], P(('groups', 'fsdp'), ('ctx', 'sub')), parts along dimension 0, may hold values from -11 to 11
- value_heads: bfloat16 [4, 2048, 512], P(('groups', 'fsdp'), ('ctx', 'sub')), parts along dimension 0, may hold values from -6 to 6
- grad_out: bfloat16 [4, 2048, 1024], P(('groups', 'fsdp'), ('ctx', 'sub')), parts along dimension 0, may hold values from -96 to 96
- doc_starts: int32 [4, 12], P(('groups', 'fsdp')), parts along dimension 0, may hold values from 0 to 2047, as said below
Outputs:
- grad_query: bfloat16 [4, 2048, 1024], P(('groups', 'fsdp'), ('ctx', 'sub')), parts along dimension 0
- grad_key: bfloat16 [4, 2048, 512], P(('groups', 'fsdp'), ('ctx', 'sub')), parts along dimension 0
- grad_value: bfloat16 [4, 2048, 512], P(('groups', 'fsdp'), ('ctx', 'sub')), parts along dimension 0
- grad_value_proj: float32 [4608, 512], P(('groups', 'fsdp')), parts along dimension 0
There are 2 independent parts, one for each index of `groups`. A program takes and returns all parts, laid end to end along the dimension named above; each array names one. Nothing has to cross between parts.
Inputs may be any that keep to these rules, and one draw needn't show every extreme that they name: `doc_starts`: each row holds the first positions of the 12 documents of one sequence in increasing order; the first is 0, every document has at least one token, and the longest has exactly 1024 tokens.
All inputs are finite; a program needn't handle non-finite values.
Results may differ from a plain program's by a relative error of at most 0.015.
Values may be sent and summed in bfloat16 or wider, within the bound.
No kernel may reach another device: no remote copies, remote signals or barrier semaphores. Data moves between devices by JAX's collectives and lax.ppermute only.
A program may use at most 64 MiB of HBM per device.

v0:
```python
import jax
import jax.numpy as jnp
from jax import lax
from jax.sharding import PartitionSpec as P

HEAD_DIM = 256
SPAN = 768


def passed_along(value, axis, steps):
    count = lax.axis_size(axis)
    first, last = (max(0, -steps), min(count, count - steps))
    return lax.ppermute(value, axis, [(source, source + steps) for source in range(first, last)])


def doc_start_of(starts, positions):
    covered = starts[None, :] <= positions[:, None]
    return jnp.max(jnp.where(covered, starts[None, :], 0), axis=1)


def attend_block(queries, key_block, value_block, grads, query_pos, key_pos, lowest):
    row_count = queries.shape[0]
    key_count = key_block.shape[0]
    groups = key_block.shape[1] // HEAD_DIM
    per_group = queries.shape[1] // key_block.shape[1]
    inv_root = HEAD_DIM ** (-0.5)
    query_four = queries.reshape(row_count, groups, per_group, HEAD_DIM)
    grad_four = grads.reshape(row_count, groups, per_group, HEAD_DIM)
    key_three = key_block.reshape(key_count, groups, HEAD_DIM)
    value_three = value_block.reshape(key_count, groups, HEAD_DIM)
    allowed = (key_pos[None, :] >= lowest[:, None]) & (key_pos[None, :] <= query_pos[:, None])

    def one_group(group):
        query_g = lax.dynamic_index_in_dim(query_four, group, 1, keepdims=False)
        grad_g = lax.dynamic_index_in_dim(grad_four, group, 1, keepdims=False)
        key_g = lax.dynamic_index_in_dim(key_three, group, 1, keepdims=False)
        value_g = lax.dynamic_index_in_dim(value_three, group, 1, keepdims=False)
        scores = (
            jnp.einsum("thd,kd->htk", query_g, key_g, preferred_element_type=jnp.float32) * inv_root
        )
        scores = jnp.where(allowed[None], scores, -1e30)
        largest = jnp.max(scores, axis=2, keepdims=True)
        raised = jnp.where(allowed[None], jnp.exp(scores - largest), 0.0)
        attn_probs = raised / jnp.sum(raised, axis=2, keepdims=True)
        grad_probs = jnp.einsum("thd,kd->htk", grad_g, value_g, preferred_element_type=jnp.float32)
        row_dot = jnp.sum(attn_probs * grad_probs, axis=2, keepdims=True)
        grad_scores = (attn_probs * (grad_probs - row_dot) * inv_root).astype(jnp.bfloat16)
        probs_low = attn_probs.astype(jnp.bfloat16)
        grad_q = jnp.einsum("htk,kd->thd", grad_scores, key_g, preferred_element_type=jnp.float32)
        grad_k = jnp.einsum("htk,thd->kd", grad_scores, query_g, preferred_element_type=jnp.float32)
        grad_v = jnp.einsum("htk,thd->kd", probs_low, grad_g, preferred_element_type=jnp.float32)
        return (grad_q, grad_k, grad_v)

    grad_q, grad_k, grad_v = lax.map(one_group, jnp.arange(groups, dtype=jnp.int32))
    grad_q = jnp.moveaxis(grad_q, 0, 1).reshape(row_count, -1)
    grad_k = jnp.moveaxis(grad_k, 0, 1).reshape(key_count, -1)
    grad_v = jnp.moveaxis(grad_v, 0, 1).reshape(key_count, -1)
    return (grad_q, grad_k, grad_v)


def body(layer_input, query_heads, key_heads, value_heads, grad_out, doc_starts):
    block_rows = query_heads.shape[1]
    window = min(SPAN, lax.axis_size(("ctx", "sub")) * block_rows // 2)
    reach_blocks = (window + block_rows - 2) // block_rows
    margin_rows = reach_blocks * block_rows
    key_count = margin_rows + block_rows
    first_row = lax.axis_index(("ctx", "sub")) * block_rows
    own_keys = key_heads[0]
    own_values = value_heads[0]
    arrived = []
    moving_k = own_keys
    moving_v = own_values
    for distance in range(reach_blocks):
        moving_k, moving_v = passed_along((moving_k, moving_v), ("ctx", "sub"), 1)
        arrived.append((moving_k, moving_v))
    arrived = arrived[::-1]
    key_span = jnp.concatenate([pair[0] for pair in arrived] + [own_keys], axis=0)
    value_span = jnp.concatenate([pair[1] for pair in arrived] + [own_values], axis=0)
    query_pos = first_row + jnp.arange(block_rows, dtype=jnp.int32)
    key_pos = first_row - margin_rows + jnp.arange(key_count, dtype=jnp.int32)
    lowest = jnp.maximum(doc_start_of(doc_starts[0], query_pos), query_pos - window + 1)
    grad_q, grad_k_span, grad_v_span = attend_block(
        query_heads[0], key_span, value_span, grad_out[0], query_pos, key_pos, lowest
    )

    def own_piece(distance):
        begin = (reach_blocks - distance) * block_rows
        return (grad_k_span[begin : begin + block_rows], grad_v_span[begin : begin + block_rows])

    total_k, total_v = own_piece(reach_blocks)
    for distance in range(reach_blocks - 1, -1, -1):
        moved_k, moved_v = (
            passed_along(total_k.astype(jnp.bfloat16), ("ctx", "sub"), -1).astype(total_k.dtype),
            passed_along(total_v.astype(jnp.bfloat16), ("ctx", "sub"), -1).astype(total_v.dtype),
        )
        piece_k, piece_v = own_piece(distance)
        total_k = moved_k + piece_k
        total_v = moved_v + piece_v
    grad_key = total_k.astype(jnp.bfloat16)
    grad_value = total_v.astype(jnp.bfloat16)
    contract = (((0,), (0,)), ((), ()))
    term_v = lax.dot_general(
        layer_input[0], grad_value, contract, preferred_element_type=jnp.float32
    )
    shard_v = lax.psum_scatter(term_v.astype(jnp.bfloat16), "fsdp", scatter_dimension=0, tiled=True)
    weight_v = lax.psum(shard_v, ("ctx", "sub")).astype(jnp.float32)
    token_scale = float(lax.axis_size("fsdp") * lax.axis_size(("ctx", "sub")) * block_rows) ** (
        -0.5
    )
    return (
        grad_q.astype(jnp.bfloat16)[None],
        grad_key[None],
        grad_value[None],
        weight_v * token_scale,
    )


def solution(mesh):
    placed = (
        P(("groups", "fsdp"), ("ctx", "sub"), None),
        P(("groups", "fsdp"), ("ctx", "sub"), None),
        P(("groups", "fsdp"), ("ctx", "sub"), None),
        P(("groups", "fsdp"), ("ctx", "sub"), None),
        P(("groups", "fsdp"), ("ctx", "sub"), None),
        P(("groups", "fsdp"), None),
    )
    return jax.shard_map(
        body,
        mesh=mesh,
        in_specs=placed,
        out_specs=(
            P(("groups", "fsdp"), ("ctx", "sub"), None),
            P(("groups", "fsdp"), ("ctx", "sub"), None),
            P(("groups", "fsdp"), ("ctx", "sub"), None),
            P(("groups", "fsdp"), None),
        ),
        check_vma=False,
    )
```

profile of v0, /device:TPU:0, one launch (start us, length us, event | category | flops | bytes accessed | tf_op | source)
XLA Modules:
  0.0 211.9 jit_solution(1971740638180802092)
XLA Ops:
  8.4 2.4 %collective-permute-start = (bf16[256,512]{0,1:T(8,128)(2,1)S(1)}, bf16[256,512]{0,1:T(8,128)(2,1)S(1)}, u32[]{:S(2)}, u32[]{:S(2)}) collective-permute-start(bf16[256,512]{0,1:T(8,128)(2,1)S(1)} %bitcast.186), channel_id=1, source_target_pairs={{0,1},{1,4},{4,5},{5,8},{8,9},{9,12},{12,13},{2,3},{3,6},{6,7},{7,... | collective-permute-start | bytes 786440 | tf_op jit(solution)/shard_map/ppermute | solution.py:13
  11.9 4.6 %collective-permute-start.3 = (bf16[256,512]{0,1:T(8,128)(2,1)S(1)}, bf16[256,512]{0,1:T(8,128)(2,1)S(1)}, u32[]{:S(2)}, u32[]{:S(2)}) collective-permute-start(bf16[256,512]{0,1:T(8,128)(2,1)S(1)} %bitcast.184), channel_id=1, source_target_pairs={{0,1},{1,4},{4,5},{5,8},{8,9},{9,12},{12,13},{2,3},{3,6},{6,7},{7,... | collective-permute-start | bytes 786440 | tf_op jit(solution)/shard_map/ppermute | solution.py:13
  16.5 2.2 %collective-permute-start.1 = (bf16[256,512]{0,1:T(8,128)(2,1)S(1)}, bf16[256,512]{0,1:T(8,128)(2,1)S(1)}, u32[]{:S(2)}, u32[]{:S(2)}) collective-permute-start(bf16[256,512]{0,1:T(8,128)(2,1)S(1)} %collective-permute-done), channel_id=1, source_target_pairs={{0,1},{1,4},{4,5},{5,8},{8,9},{9,12},{12,13},{2,3},{3,6},{6,7},{7,... | collective-permute-start | bytes 786440 | tf_op jit(solution)/shard_map/ppermute | solution.py:13
  18.7 4.4 %collective-permute-start.4 = (bf16[256,512]{0,1:T(8,128)(2,1)S(1)}, bf16[256,512]{0,1:T(8,128)(2,1)S(1)}, u32[]{:S(2)}, u32[]{:S(2)}) collective-permute-start(bf16[256,512]{0,1:T(8,128)(2,1)S(1)} %collective-permute-done.3), channel_id=1, source_target_pairs={{0,1},{1,4},{4,5},{5,8},{8,9},{9,12},{12,13},{2,3},{3,6},{6,7},{7,... | collective-permute-start | bytes 786440 | tf_op jit(solution)/shard_map/ppermute | solution.py:13
  23.9 3.7 %collective-permute-start.2 = (bf16[256,512]{0,1:T(8,128)(2,1)S(1)}, bf16[256,512]{0,1:T(8,128)(2,1)}, u32[]{:S(2)}, u32[]{:S(2)}) collective-permute-start(bf16[256,512]{0,1:T(8,128)(2,1)S(1)} %collective-permute-done.1), channel_id=1, source_target_pairs={{0,1},{1,4},{4,5},{5,8},{8,9},{9,12},{12,13},{2,3},{3,6},{6,7},{7,... | collective-permute-start | bytes 786440 | tf_op jit(solution)/shard_map/ppermute | solution.py:13
  27.6 3.2 %collective-permute-start.5 = (bf16[256,512]{0,1:T(8,128)(2,1)S(1)}, bf16[256,512]{0,1:T(8,128)(2,1)S(1)}, u32[]{:S(2)}, u32[]{:S(2)}) collective-permute-start(bf16[256,512]{0,1:T(8,128)(2,1)S(1)} %collective-permute-done.4), channel_id=1, source_target_pairs={{0,1},{1,4},{4,5},{5,8},{8,9},{9,12},{12,13},{2,3},{3,6},{6,7},{7,... | collective-permute-start | bytes 786440 | tf_op jit(solution)/shard_map/ppermute | solution.py:13
  30.8 2.1 copy.73
  33.9 2.1 pad_maximum_fusion
  37.1 37.4 %while.15 = (s32[]{:T(128)}, bf16[2,256,2,256]{1,3,2,0:T(8,128)(2,1)}, f32[2,1024,256]{2,1,0:T(8,128)}, f32[2,1024,256]{2,1,0:T(8,128)}, s32[2]{0:T(128)S(1)}, /...) while((s32[]{:T(128)}, ...), condition=%wide.region_5.6_spmd.clone, body=%wide.region_1.5_spmd.clone.sunk | while | flops 1353977856 | bytes 29120200 | solution.py:54
  39.9 3.5 %fusion.90 = (f32[2,256]{1,0:T(2,128)S(1)}, f32[2,256,1024]{1,2,0:T(8,128)}) fusion(pred[256,1024]{0,1:T(8,128)(4,1)S(1)} %compare_and_fusion.2, bf16[256,2,2,256]{0,3,2,1:T(8,128)(2,1)} %get-tuple-element.287, s32[]{:T(128)S(6)} %select_n.34, bf16[1024,2,256]{0,2,1:T(8,128)(2,1)} %get-tuple-element.286), kind=kOutput, calls=%fused_computation.80.clone.1 | convolution fusion | flops 271057920 | bytes 3410944 | tf_op jit(solution)/shard_map/while/body/eval_jaxpr/sub | solution.py:43
  43.4 1.6 fusion.89
  45.0 3.9 %fusion.92 = f32[2,1024,256]{2,1,0:T(8,128)} fusion(f32[2,1024,256]{2,1,0:T(8,128)} %get-tuple-element.268, s32[]{:T(128)} %get-tuple-element.266, f32[1024,256,2]{1,0,2:T(8,128)S(1)} %fusion.89, bf16[256,2,2,256]{0,3,2,1:T(8,128)(2,1)} %get-tuple-element.287, s32[]{:T(128)S(6)} %select_n.34, f32[2,256,1024]{1,2,0:T(8,128)} %get-tuple-element.249, ...), kind=kOutput, calls=%fused_computation.14.clone.1 | convolution fusion | flops 272107008 | bytes 9703940 | tf_op jit(solution)/shard_map/while/body/eval_jaxpr/htk,thd->kd/dot_general | solution.py:50
  48.9 3.0 %fusion.93 = f32[2,1024,256]{2,1,0:T(8,128)} fusion(f32[2,1024,256]{2,1,0:T(8,128)} %get-tuple-element.269, s32[]{:T(128)} %get-tuple-element.266, bf16[256,2,2,256]{0,3,2,1:T(8,128)(2,1)} %get-tuple-element.289, s32[]{:T(128)S(6)} %select_n.34, f32[2,256,1024]{1,2,0:T(8,128)} %get-tuple-element.249, f32[2,256]{1,0:T(2,128)S(1)} %get-tuple-element.250), kind=kOutput, calls=%fused_computation.12.clone.1 | convolution fusion | flops 269484032 | bytes 3410436 | tf_op jit(solution)/shard_map/while/body/eval_jaxpr/htk,thd->kd/dot_general | solution.py:51
  51.9 3.9 %fusion.91 = bf16[2,256,2,256]{1,3,2,0:T(8,128)(2,1)} fusion(bf16[2,256,2,256]{1,3,2,0:T(8,128)(2,1)} %get-tuple-element.267, s32[]{:T(128)} %get-tuple-element.266, f32[1024,256,2]{1,0,2:T(8,128)S(1)} %fusion.89, bf16[1024,2,256]{0,2,1:T(8,128)(2,1)} %get-tuple-element.286, s32[]{:T(128)S(6)} %select_n.34, f32[2,256,1024]{1,2,0:T(8,128)} %get-tuple-element.249, ...), kind=kOutput, calls=%fused_computation.16.clone.1 | convolution fusion | flops 272107008 | bytes 9441796 | tf_op jit(solution)/shard_map/while/body/eval_jaxpr/htk,kd->thd/dot_general | solution.py:49
  58.6 3.5 %fusion.90 = (f32[2,256]{1,0:T(2,128)S(1)}, f32[2,256,1024]{1,2,0:T(8,128)}) fusion(pred[256,1024]{0,1:T(8,128)(4,1)S(1)} %compare_and_fusion.2, bf16[256,2,2,256]{0,3,2,1:T(8,128)(2,1)} %get-tuple-element.287, s32[]{:T(128)S(6)} %select_n.34, bf16[1024,2,256]{0,2,1:T(8,128)(2,1)} %get-tuple-element.286), kind=kOutput, calls=%fused_computation.80.clone.1 | convolution fusion | flops 271057920 | bytes 3410944 | tf_op jit(solution)/shard_map/while/body/eval_jaxpr/sub | solution.py:43
  62.1 1.6 fusion.89
  63.6 4.0 %fusion.92 = f32[2,1024,256]{2,1,0:T(8,128)} fusion(f32[2,1024,256]{2,1,0:T(8,128)} %get-tuple-element.268, s32[]{:T(128)} %get-tuple-element.266, f32[1024,256,2]{1,0,2:T(8,128)S(1)} %fusion.89, bf16[256,2,2,256]{0,3,2,1:T(8,128)(2,1)} %get-tuple-element.287, s32[]{:T(128)S(6)} %select_n.34, f32[2,256,1024]{1,2,0:T(8,128)} %get-tuple-element.249, ...), kind=kOutput, calls=%fused_computation.14.clone.1 | convolution fusion | flops 272107008 | bytes 9703940 | tf_op jit(solution)/shard_map/while/body/eval_jaxpr/htk,thd->kd/dot_general | solution.py:50
  67.6 3.0 %fusion.93 = f32[2,1024,256]{2,1,0:T(8,128)} fusion(f32[2,1024,256]{2,1,0:T(8,128)} %get-tuple-element.269, s32[]{:T(128)} %get-tuple-element.266, bf16[256,2,2,256]{0,3,2,1:T(8,128)(2,1)} %get-tuple-element.289, s32[]{:T(128)S(6)} %select_n.34, f32[2,256,1024]{1,2,0:T(8,128)} %get-tuple-element.249, f32[2,256]{1,0:T(2,128)S(1)} %get-tuple-element.250), kind=kOutput, calls=%fused_computation.12.clone.1 | convolution fusion | flops 269484032 | bytes 3410436 | tf_op jit(solution)/shard_map/while/body/eval_jaxpr/htk,thd->kd/dot_general | solution.py:51
  70.7 3.9 %fusion.91 = bf16[2,256,2,256]{1,3,2,0:T(8,128)(2,1)} fusion(bf16[2,256,2,256]{1,3,2,0:T(8,128)(2,1)} %get-tuple-element.267, s32[]{:T(128)} %get-tuple-element.266, f32[1024,256,2]{1,0,2:T(8,128)S(1)} %fusion.89, bf16[1024,2,256]{0,2,1:T(8,128)(2,1)} %get-tuple-element.286, s32[]{:T(128)S(6)} %select_n.34, f32[2,256,1024]{1,2,0:T(8,128)} %get-tuple-element.249, ...), kind=kOutput, calls=%fused_computation.16.clone.1 | convolution fusion | flops 272107008 | bytes 9441796 | tf_op jit(solution)/shard_map/while/body/eval_jaxpr/htk,kd->thd/dot_general | solution.py:49
  76.9 1.5 slice_bitcast_fusion.2
  81.1 6.3 %collective-permute-done.10 = bf16[256,512]{1,0:T(8,128)(2,1)S(1)} collective-permute-done((bf16[256,512]{1,0:T(8,128)(2,1)S(1)}, bf16[256,512]{1,0:T(8,128)(2,1)S(1)}, u32[]{:S(2)}, u32[]{:S(2)}) %collective-permute-start.10) | collective-permute-done | bytes 262176 | tf_op jit(solution)/shard_map/ppermute | solution.py:13
  88.9 6.3 %collective-permute-done.11 = bf16[256,512]{1,0:T(8,128)(2,1)S(1)} collective-permute-done((bf16[256,512]{1,0:T(8,128)(2,1)S(1)}, bf16[256,512]{1,0:T(8,128)(2,1)S(1)}, u32[]{:S(2)}, u32[]{:S(2)}) %collective-permute-start.11) | collective-permute-done | bytes 262176 | tf_op jit(solution)/shard_map/ppermute | solution.py:13
  96.7 2.4 %copy.92 = bf16[2304,512]{1,0:T(8,128)(2,1)} copy(bf16[2304,512]{0,1:T(8,128)(2,1)S(1)} %fusion.57) | data formatting | bytes 4718592
  101.7 1.5 slice_bitcast_fusion.5
  103.2 4.9 %collective-permute-done.6 = bf16[256,512]{1,0:T(8,128)(2,1)S(1)} collective-permute-done((bf16[256,512]{1,0:T(8,128)(2,1)S(1)}, bf16[256,512]{1,0:T(8,128)(2,1)S(1)}, u32[]{:S(2)}, u32[]{:S(2)}) %collective-permute-start.6) | collective-permute-done | bytes 262176 | tf_op jit(solution)/shard_map/ppermute | solution.py:13
  110.2 28.5 %reduce-scatter.4.cloned.1.call-done = bf16[1152,512]{1,0:T(8,128)(2,1)} async-done(((bf16[2304,512]{1,0:T(8,128)(2,1)}), bf16[1152,512]{1,0:T(8,128)(2,1)}) %reduce-scatter.4.cloned.1.call-update) | async-done | bytes 1179664
  138.7 2.4 %copy.93 = bf16[1152,512]{0,1:T(8,128)(2,1)} copy(bf16[1152,512]{1,0:T(8,128)(2,1)} %reduce-scatter.4.cloned.1.call-done) | data formatting | bytes 2359296
  141.1 1.8 add_convert_fusion.4
  146.7 1.7 fusion.59
  148.4 53.2 %all-reduce.2.cloned.1.call-done = bf16[1152,512]{0,1:T(8,128)(2,1)} async-done(((bf16[1152,512]{0,1:T(8,128)(2,1)}), bf16[1152,512]{0,1:T(8,128)(2,1)}) %all-reduce.2.cloned.1.call-update) | async-done | bytes 1179664 | tf_op jit(solution)/shard_map/psum | solution.py:106
  201.6 1.4 convert_multiply_fusion
  203.1 2.0 copy.87
  (65 shorter events, 23.3 us)
Async XLA Ops:
  7.2 88.7 %copy-start = (bf16[1,256,2304]{2,1,0:T(8,128)(2,1)S(1)}, bf16[1,256,2304]{2,1,0:T(8,128)(2,1)}, u32[]{:S(2)}) copy-start(bf16[1,256,2304]{2,1,0:T(8,128)(2,1)} %param.8) | copy-start | bytes 3538948
  7.2 25.7 %copy-start.5 = (bf16[1,256,1024]{2,1,0:T(8,128)(2,1)S(1)}, bf16[1,256,1024]{2,1,0:T(8,128)(2,1)}, u32[]{:S(2)}) copy-start(bf16[1,256,1024]{2,1,0:T(8,128)(2,1)} %param.9) | copy-start | bytes 1572868
  7.2 131.5 %reduce-scatter.4.cloned.1.call-start = ((), (), s32[]{:S(2)}) async-start(), calls=%async_computation.2 | async-start | bytes 3538944
  8.4 8.1 %collective-permute-start = (bf16[256,512]{0,1:T(8,128)(2,1)S(1)}, bf16[256,512]{0,1:T(8,128)(2,1)S(1)}, u32[]{:S(2)}, u32[]{:S(2)}) collective-permute-start(bf16[256,512]{0,1:T(8,128)(2,1)S(1)} %bitcast.186), channel_id=1, source_target_pairs={{0,1},{1,4},{4,5},{5,8},{8,9},{9,12},{12,13},{2,3},{3,6},{6,7},{7,... | collective-permute-start | bytes 786440 | tf_op jit(solution)/shard_map/ppermute | solution.py:13
  11.9 6.8 %collective-permute-start.3 = (bf16[256,512]{0,1:T(8,128)(2,1)S(1)}, bf16[256,512]{0,1:T(8,128)(2,1)S(1)}, u32[]{:S(2)}, u32[]{:S(2)}) collective-permute-start(bf16[256,512]{0,1:T(8,128)(2,1)S(1)} %bitcast.184), channel_id=1, source_target_pairs={{0,1},{1,4},{4,5},{5,8},{8,9},{9,12},{12,13},{2,3},{3,6},{6,7},{7,... | collective-permute-start | bytes 786440 | tf_op jit(solution)/shard_map/ppermute | solution.py:13
  16.5 7.4 %collective-permute-start.1 = (bf16[256,512]{0,1:T(8,128)(2,1)S(1)}, bf16[256,512]{0,1:T(8,128)(2,1)S(1)}, u32[]{:S(2)}, u32[]{:S(2)}) collective-permute-start(bf16[256,512]{0,1:T(8,128)(2,1)S(1)} %collective-permute-done), channel_id=1, source_target_pairs={{0,1},{1,4},{4,5},{5,8},{8,9},{9,12},{12,13},{2,3},{3,6},{6,7},{7,... | collective-permute-start | bytes 786440 | tf_op jit(solution)/shard_map/ppermute | solution.py:13
  18.7 8.9 %collective-permute-start.4 = (bf16[256,512]{0,1:T(8,128)(2,1)S(1)}, bf16[256,512]{0,1:T(8,128)(2,1)S(1)}, u32[]{:S(2)}, u32[]{:S(2)}) collective-permute-start(bf16[256,512]{0,1:T(8,128)(2,1)S(1)} %collective-permute-done.3), channel_id=1, source_target_pairs={{0,1},{1,4},{4,5},{5,8},{8,9},{9,12},{12,13},{2,3},{3,6},{6,7},{7,... | collective-permute-start | bytes 786440 | tf_op jit(solution)/shard_map/ppermute | solution.py:13
  23.9 10.0 %collective-permute-start.2 = (bf16[256,512]{0,1:T(8,128)(2,1)S(1)}, bf16[256,512]{0,1:T(8,128)(2,1)}, u32[]{:S(2)}, u32[]{:S(2)}) collective-permute-start(bf16[256,512]{0,1:T(8,128)(2,1)S(1)} %collective-permute-done.1), channel_id=1, source_target_pairs={{0,1},{1,4},{4,5},{5,8},{8,9},{9,12},{12,13},{2,3},{3,6},{6,7},{7,... | collective-permute-start | bytes 786440 | tf_op jit(solution)/shard_map/ppermute | solution.py:13
  27.6 8.4 %collective-permute-start.5 = (bf16[256,512]{0,1:T(8,128)(2,1)S(1)}, bf16[256,512]{0,1:T(8,128)(2,1)S(1)}, u32[]{:S(2)}, u32[]{:S(2)}) collective-permute-start(bf16[256,512]{0,1:T(8,128)(2,1)S(1)} %collective-permute-done.4), channel_id=1, source_target_pairs={{0,1},{1,4},{4,5},{5,8},{8,9},{9,12},{12,13},{2,3},{3,6},{6,7},{7,... | collective-permute-start | bytes 786440 | tf_op jit(solution)/shard_map/ppermute | solution.py:13
  75.6 4.0 %collective-permute-start.9 = (bf16[256,512]{1,0:T(8,128)(2,1)S(1)}, bf16[256,512]{1,0:T(8,128)(2,1)S(1)}, u32[]{:S(2)}, u32[]{:S(2)}) collective-permute-start(bf16[256,512]{1,0:T(8,128)(2,1)S(1)} %bitcast.189), channel_id=1, source_target_pairs={{1,0},{4,1},{5,4},{8,5},{9,8},{12,9},{13,12},{3,2},{6,3},{7,6},{10... | collective-permute-start | bytes 786440 | tf_op jit(solution)/shard_map/ppermute | solution.py:13
  79.7 7.7 %collective-permute-start.10 = (bf16[256,512]{1,0:T(8,128)(2,1)S(1)}, bf16[256,512]{1,0:T(8,128)(2,1)S(1)}, u32[]{:S(2)}, u32[]{:S(2)}) collective-permute-start(bf16[256,512]{1,0:T(8,128)(2,1)S(1)} %add_convert_fusion.2), channel_id=1, source_target_pairs={{1,0},{4,1},{5,4},{8,5},{9,8},{12,9},{13,12},{3,2},{6,3},{7,6},{10... | collective-permute-start | bytes 786440 | tf_op jit(solution)/shard_map/ppermute | solution.py:13
  87.5 7.7 %collective-permute-start.11 = (bf16[256,512]{1,0:T(8,128)(2,1)S(1)}, bf16[256,512]{1,0:T(8,128)(2,1)S(1)}, u32[]{:S(2)}, u32[]{:S(2)}) collective-permute-start(bf16[256,512]{1,0:T(8,128)(2,1)S(1)} %add_convert_fusion.1), channel_id=1, source_target_pairs={{1,0},{4,1},{5,4},{8,5},{9,8},{12,9},{13,12},{3,2},{6,3},{7,6},{10... | collective-permute-start | bytes 786440 | tf_op jit(solution)/shard_map/ppermute | solution.py:13
  88.9 6.3 %copy-start.1 = (f32[2,32,8,256]{3,2,0,1:T(8,128)}, f32[2,32,8,256]{3,2,0,1:T(8,128)S(1)}, u32[]{:S(2)}) copy-start(f32[2,32,8,256]{3,2,0,1:T(8,128)S(1)} %copy.105) | copy-start | bytes 1572868
  95.2 0.7 copy-start.3
  99.2 102.4 %all-reduce.2.cloned.1.call-start = ((), (), s32[]{:S(2)}) async-start(), calls=%async_computation.1 | async-start | bytes 2359296 | tf_op jit(solution)/shard_map/psum | solution.py:106
  100.4 7.7 %collective-permute-start.6 = (bf16[256,512]{1,0:T(8,128)(2,1)S(1)}, bf16[256,512]{1,0:T(8,128)(2,1)S(1)}, u32[]{:S(2)}, u32[]{:S(2)}) collective-permute-start(bf16[256,512]{1,0:T(8,128)(2,1)S(1)} %bitcast.190), channel_id=1, source_target_pairs={{1,0},{4,1},{5,4},{8,5},{9,8},{12,9},{13,12},{3,2},{6,3},{7,6},{10... | collective-permute-start | bytes 786440 | tf_op jit(solution)/shard_map/ppermute | solution.py:13
  108.8 32.3 %collective-permute-start.7 = (bf16[256,512]{1,0:T(8,128)(2,1)}, bf16[256,512]{1,0:T(8,128)(2,1)}, u32[]{:S(2)}, u32[]{:S(2)}) collective-permute-start(bf16[256,512]{1,0:T(8,128)(2,1)} %add_convert_fusion.5), channel_id=1, source_target_pairs={{1,0},{4,1},{5,4},{8,5},{9,8},{12,9},{13,12},{3,2},{6,3},{7,6},{10... | collective-permute-start | bytes 786440 | tf_op jit(solution)/shard_map/ppermute | solution.py:13
  141.1 3.2 %copy-start.6 = (bf16[2,256,2,256]{1,3,2,0:T(8,128)(2,1)S(1)}, bf16[2,256,2,256]{1,3,2,0:T(8,128)(2,1)}, u32[]{:S(2)}) copy-start(bf16[2,256,2,256]{1,3,2,0:T(8,128)(2,1)} %get-tuple-element.58) | copy-start | bytes 1572868
  141.1 4.2 %copy-start.2 = (f32[2,32,8,256]{3,2,0,1:T(8,128)S(1)}, f32[2,32,8,256]{3,2,0,1:T(8,128)}, u32[]{:S(2)}) copy-start(f32[2,32,8,256]{3,2,0,1:T(8,128)} %copy-done.1) | copy-start | bytes 1572868
  141.1 4.2 %copy-start.4 = (bf16[256,512]{1,0:T(8,128)(2,1)S(1)}, bf16[256,512]{1,0:T(8,128)(2,1)}, u32[]{:S(2)}) copy-start(bf16[256,512]{1,0:T(8,128)(2,1)} %copy-done.3) | copy-start | bytes 786436
  142.9 3.8 %collective-permute-start.8 = (bf16[256,512]{1,0:T(8,128)(2,1)}, bf16[256,512]{1,0:T(8,128)(2,1)}, u32[]{:S(2)}, u32[]{:S(2)}) collective-permute-start(bf16[256,512]{1,0:T(8,128)(2,1)} %add_convert_fusion.4), channel_id=1, source_target_pairs={{1,0},{4,1},{5,4},{8,5},{9,8},{12,9},{13,12},{3,2},{6,3},{7,6},{10... | collective-permute-start | bytes 786440 | tf_op jit(solution)/shard_map/ppermute | solution.py:13
Sparse Core Ops, SparseCore 0:
  99.3 39.3 reduce-scatter.3
  141.7 59.8 all-reduce.1
where the time goes:
time: 213 us; the launch traced here: 212 us
  waiting for transfers between devices  101 us (47%)
  matrix products  32.6 us (15%)
  starting transfers between devices  28.2 us (13%)
  local copies, waits for them, and re-layouts  20.5 us (10%)
  between operations  14.4 us (7%)
  other arithmetic  11.2 us (5%)
  loops' own time  3.92 us (2%)
    psum x1, waiting for transfers between devices, body(): weight_v = lax.psum(shard_v, ('ctx', 'sub')).astype(jnp.float32)  53.2 us
    unnamed x3, waiting for transfers between devices  28.5 us
    ppermute x12, starting transfers between devices, passed_along(): lax.ppermute(value, axis, [(source, source + steps) for source in range(f...  28.2 us
    ppermute x12, waiting for transfers between devices, passed_along(): lax.ppermute(value, axis, [(source, source + steps) for source in range(f...  19.3 us
    unnamed x25, local copies, waits for them, and re-layouts  17.9 us
    dot_general x2, matrix products, one_group(): jnp.einsum('htk,thd->kd', grad_scores, query_g, preferred_element_type=jn...  7.91 us
    dot_general x2, matrix products, one_group(): jnp.einsum('htk,kd->thd', grad_scores, key_g, preferred_element_type=jnp....  7.74 us
    sub x2, matrix products, one_group(): raised = jnp.where(allowed[None], jnp.exp(scores - largest), 0.0)  6.91 us
  transfers between devices with their start and end apart: 14, of which 7 were waited for; matrix products, arithmetic and copies ran while one was open for 9% of the time, Pallas kernels for 0%

commit v1 on v0

--- a/solution.py
+++ b/solution.py
@@ -103,7 +103,7 @@
         layer_input[0], grad_value, contract, preferred_element_type=jnp.float32
     )
     shard_v = lax.psum_scatter(term_v.astype(jnp.bfloat16), "fsdp", scatter_dimension=0, tiled=True)
-    weight_v = lax.psum(shard_v, ("ctx", "sub")).astype(jnp.float32)
+    weight_v = jnp.sum(lax.all_gather(shard_v, ("ctx", "sub")), axis=0).astype(jnp.float32)
     token_scale = float(lax.axis_size("fsdp") * lax.axis_size(("ctx", "sub")) * block_rows) ** (
         -0.5
     )

time: 213 us -> 267 us (1.25)
  waiting for transfers between devices: 101 us -> 139 us
  local copies, waits for them, and re-layouts: 20.5 us -> 29.3 us
  other arithmetic: 11.2 us -> 18.8 us
    all_gather x0 -> x1, waiting for transfers between devices: none -> 65.9 us  [body(): lax.all_gather(shard_v, ('ctx', 'sub'))]
    psum x1 -> x0, waiting for transfers between devices: 53.2 us -> none  [body(): weight_v = lax.psum(shard_v, ('ctx', 'sub')).astype(jnp.float32)]
    ppermute x12, waiting for transfers between devices: 19.3 us -> 33.8 us  [passed_along(): lax.ppermute(value, axis, [(source, source + steps) for source in range(f...]
    reduce_sum x0 -> x1, other arithmetic: none -> 11 us  [body(): jnp.sum(lax.all_gather(shard_v, ('ctx', 'sub')), axis=0).astype(jnp.float32)]
    unnamed x3, waiting for transfers between devices: 28.5 us -> 39.5 us
    unnamed x25 -> x26, local copies, waits for them, and re-layouts: 17.9 us -> 26.6 us
  transfers between devices with their start and end apart: 14 -> 14, of which waited for: 7 -> 8; matrix products, arithmetic and copies ran while one was open for 9% -> 5% of each run, Pallas kernels for 0% -> 0%
where the time goes in v1:
time: 267 us; the launch traced here: 266 us
  waiting for transfers between devices  139 us (52%)
  matrix products  30.7 us (11%)
  local copies, waits for them, and re-layouts  29.3 us (11%)
  starting transfers between devices  29.3 us (11%)
  other arithmetic  18.8 us (7%)
  between operations  14.4 us (5%)
  loops' own time  3.96 us (1%)
    all_gather x1, waiting for transfers between devices, body(): lax.all_gather(shard_v, ('ctx', 'sub'))  65.9 us
    unnamed x3, waiting for transfers between devices  39.5 us
    ppermute x12, waiting for transfers between devices, passed_along(): lax.ppermute(value, axis, [(source, source + steps) for source in range(f...  33.8 us
    ppermute x12, starting transfers between devices, passed_along(): lax.ppermute(value, axis, [(source, source + steps) for source in range(f...  29.2 us
    unnamed x26, local copies, waits for them, and re-layouts  26.6 us
    reduce_sum x1, other arithmetic, body(): jnp.sum(lax.all_gather(shard_v, ('ctx', 'sub')), axis=0).astype(jnp.float32)  11 us
    dot_general x2, matrix products, one_group(): jnp.einsum('htk,thd->kd', grad_scores, query_g, preferred_element_type=jn...  7.86 us
    dot_general x2, matrix products, one_group(): jnp.einsum('htk,kd->thd', grad_scores, key_g, preferred_element_type=jnp....  7.76 us
  transfers between devices with their start and end apart: 14, of which 8 were waited for; matrix products, arithmetic and copies ran while one was open for 5% of the time, Pallas kernels for 0%

profile of v1, /device:TPU:0, one launch (start us, length us, event | category | flops | bytes accessed | tf_op | source)
XLA Modules:
  0.0 265.7 jit_solution(13422360659507364431)
XLA Ops:
  8.4 2.4 collective-permute-start.3
  11.9 4.6 %collective-permute-start = (bf16[256,512]{0,1:T(8,128)(2,1)S(1)}, bf16[256,512]{0,1:T(8,128)(2,1)S(1)}, u32[]{:S(2)}, u32[]{:S(2)}) collective-permute-start(bf16[256,512]{0,1:T(8,128)(2,1)S(1)} %bitcast.190), channel_id=1, source_target_pairs={{0,1},{1,4},{4,5},{5,8},{8,9},{9,12},{12,13},{2,3},{3,6},{6,7},{7,... | collective-permute-start | bytes 786440 | tf_op jit(solution)/shard_map/ppermute | solution.py:13
  16.5 2.9 %collective-permute-start.4 = (bf16[256,512]{0,1:T(8,128)(2,1)S(1)}, bf16[256,512]{0,1:T(8,128)(2,1)}, u32[]{:S(2)}, u32[]{:S(2)}) collective-permute-start(bf16[256,512]{0,1:T(8,128)(2,1)S(1)} %collective-permute-done.3), channel_id=1, source_target_pairs={{0,1},{1,4},{4,5},{5,8},{8,9},{9,12},{12,13},{2,3},{3,6},{6,7},{7,... | collective-permute-start | bytes 786440 | tf_op jit(solution)/shard_map/ppermute | solution.py:13
  19.4 3.7 %collective-permute-start.1 = (bf16[256,512]{0,1:T(8,128)(2,1)S(1)}, bf16[256,512]{0,1:T(8,128)(2,1)S(1)}, u32[]{:S(2)}, u32[]{:S(2)}) collective-permute-start(bf16[256,512]{0,1:T(8,128)(2,1)S(1)} %collective-permute-done), channel_id=1, source_target_pairs={{0,1},{1,4},{4,5},{5,8},{8,9},{9,12},{12,13},{2,3},{3,6},{6,7},{7,... | collective-permute-start | bytes 786440 | tf_op jit(solution)/shard_map/ppermute | solution.py:13
  23.9 3.7 %collective-permute-start.5 = (bf16[256,512]{0,1:T(8,128)(2,1)}, bf16[256,512]{0,1:T(8,128)(2,1)}, u32[]{:S(2)}, u32[]{:S(2)}) collective-permute-start(bf16[256,512]{0,1:T(8,128)(2,1)} %collective-permute-done.4), channel_id=1, source_target_pairs={{0,1},{1,4},{4,5},{5,8},{8,9},{9,12},{12,13},{2,3},{3,6},{6,7},{7,... | collective-permute-start | bytes 786440 | tf_op jit(solution)/shard_map/ppermute | solution.py:13
  27.6 4.0 %collective-permute-start.2 = (bf16[256,512]{0,1:T(8,128)(2,1)S(1)}, bf16[256,512]{0,1:T(8,128)(2,1)}, u32[]{:S(2)}, u32[]{:S(2)}) collective-permute-start(bf16[256,512]{0,1:T(8,128)(2,1)S(1)} %collective-permute-done.1), channel_id=1, source_target_pairs={{0,1},{1,4},{4,5},{5,8},{8,9},{9,12},{12,13},{2,3},{3,6},{6,7},{7,... | collective-permute-start | bytes 786440 | tf_op jit(solution)/shard_map/ppermute | solution.py:13
  33.9 2.1 pad_maximum_fusion.1
  37.1 35.7 %while.15 = (s32[]{:T(128)}, bf16[2,256,2,256]{1,3,2,0:T(8,128)(2,1)}, f32[2,1024,256]{2,1,0:T(8,128)}, f32[2,1024,256]{2,1,0:T(8,128)}, s32[2]{0:T(128)S(1)}, /...) while((s32[]{:T(128)}, ...), condition=%wide.region_5.6_spmd.clone, body=%wide.region_1.5_spmd.clone.sunk | while | flops 1353977856 | bytes 41701704 | solution.py:54
  40.1 2.4 fusion.90
  42.4 1.6 fusion.89
  44.0 3.9 %fusion.91 = bf16[2,256,2,256]{1,3,2,0:T(8,128)(2,1)} fusion(bf16[2,256,2,256]{1,3,2,0:T(8,128)(2,1)} %get-tuple-element.259, s32[]{:T(128)S(6)} %copy.112, f32[1024,256,2]{1,0,2:T(8,128)S(1)} %fusion.89, bf16[1024,2,256]{0,2,1:T(8,128)(2,1)} %copy-done.3, s32[]{:T(128)S(6)} %select_n.34, f32[2,256,1024]{1,2,0:T(8,128)} %get-tuple-element.241, ...), kind=kOutput, calls=%fused_computation.16.clone.1 | convolution fusion | flops 272107008 | bytes 9441288 | tf_op jit(solution)/shard_map/while/body/eval_jaxpr/htk,kd->thd/dot_general | solution.py:49
  47.9 3.9 %fusion.92 = f32[2,1024,256]{2,1,0:T(8,128)} fusion(f32[2,1024,256]{2,1,0:T(8,128)} %get-tuple-element.260, s32[]{:T(128)S(6)} %copy.112, f32[1024,256,2]{1,0,2:T(8,128)S(1)} %fusion.89, bf16[256,2,2,256]{0,3,2,1:T(8,128)(2,1)} %copy-done.8, s32[]{:T(128)S(6)} %select_n.34, f32[2,256,1024]{1,2,0:T(8,128)} %get-tuple-element.241, ...), kind=kOutput, calls=%fused_computation.14.clone.1 | convolution fusion | flops 272107008 | bytes 9703432 | tf_op jit(solution)/shard_map/while/body/eval_jaxpr/htk,thd->kd/dot_general | solution.py:50
  51.8 3.2 %fusion.93 = f32[2,1024,256]{2,1,0:T(8,128)} fusion(f32[2,1024,256]{2,1,0:T(8,128)} %get-tuple-element.261, s32[]{:T(128)S(6)} %copy.112, bf16[256,2,2,256]{0,3,2,1:T(8,128)(2,1)} %get-tuple-element.281, s32[]{:T(128)S(6)} %select_n.34, f32[2,256,1024]{1,2,0:T(8,128)} %get-tuple-element.241, f32[2,256]{1,0:T(2,128)S(1)} %get-tuple-element.242), kind=kOutput, calls=%fused_computation.12.clone.1 | convolution fusion | flops 269484032 | bytes 3409928 | tf_op jit(solution)/shard_map/while/body/eval_jaxpr/htk,thd->kd/dot_general | solution.py:51
  57.9 2.4 fusion.90
  60.3 1.6 fusion.89
  61.9 3.9 %fusion.91 = bf16[2,256,2,256]{1,3,2,0:T(8,128)(2,1)} fusion(bf16[2,256,2,256]{1,3,2,0:T(8,128)(2,1)} %get-tuple-element.259, s32[]{:T(128)S(6)} %copy.112, f32[1024,256,2]{1,0,2:T(8,128)S(1)} %fusion.89, bf16[1024,2,256]{0,2,1:T(8,128)(2,1)} %copy-done.3, s32[]{:T(128)S(6)} %select_n.34, f32[2,256,1024]{1,2,0:T(8,128)} %get-tuple-element.241, ...), kind=kOutput, calls=%fused_computation.16.clone.1 | convolution fusion | flops 272107008 | bytes 9441288 | tf_op jit(solution)/shard_map/while/body/eval_jaxpr/htk,kd->thd/dot_general | solution.py:49
  65.7 3.9 %fusion.92 = f32[2,1024,256]{2,1,0:T(8,128)} fusion(f32[2,1024,256]{2,1,0:T(8,128)} %get-tuple-element.260, s32[]{:T(128)S(6)} %copy.112, f32[1024,256,2]{1,0,2:T(8,128)S(1)} %fusion.89, bf16[256,2,2,256]{0,3,2,1:T(8,128)(2,1)} %copy-done.8, s32[]{:T(128)S(6)} %select_n.34, f32[2,256,1024]{1,2,0:T(8,128)} %get-tuple-element.241, ...), kind=kOutput, calls=%fused_computation.14.clone.1 | convolution fusion | flops 272107008 | bytes 9703432 | tf_op jit(solution)/shard_map/while/body/eval_jaxpr/htk,thd->kd/dot_general | solution.py:50
  69.7 3.1 %fusion.93 = f32[2,1024,256]{2,1,0:T(8,128)} fusion(f32[2,1024,256]{2,1,0:T(8,128)} %get-tuple-element.261, s32[]{:T(128)S(6)} %copy.112, bf16[256,2,2,256]{0,3,2,1:T(8,128)(2,1)} %get-tuple-element.281, s32[]{:T(128)S(6)} %select_n.34, f32[2,256,1024]{1,2,0:T(8,128)} %get-tuple-element.241, f32[2,256]{1,0:T(2,128)S(1)} %get-tuple-element.242), kind=kOutput, calls=%fused_computation.12.clone.1 | convolution fusion | flops 269484032 | bytes 3409928 | tf_op jit(solution)/shard_map/while/body/eval_jaxpr/htk,thd->kd/dot_general | solution.py:51
  75.2 1.5 slice_bitcast_fusion.2
  78.8 6.1 %collective-permute-done.10 = bf16[256,512]{1,0:T(8,128)(2,1)S(1)} collective-permute-done((bf16[256,512]{1,0:T(8,128)(2,1)S(1)}, bf16[256,512]{1,0:T(8,128)(2,1)S(1)}, u32[]{:S(2)}, u32[]{:S(2)}) %collective-permute-start.10) | collective-permute-done | bytes 262176 | tf_op jit(solution)/shard_map/ppermute | solution.py:13
  86.4 6.3 %collective-permute-done.11 = bf16[256,512]{1,0:T(8,128)(2,1)S(1)} collective-permute-done((bf16[256,512]{1,0:T(8,128)(2,1)S(1)}, bf16[256,512]{1,0:T(8,128)(2,1)S(1)}, u32[]{:S(2)}, u32[]{:S(2)}) %collective-permute-start.11) | collective-permute-done | bytes 262176 | tf_op jit(solution)/shard_map/ppermute | solution.py:13
  94.3 2.4 copy.90
  96.8 39.5 %reduce-scatter.4.cloned.1.call-done = bf16[1152,512]{1,0:T(8,128)(2,1)} async-done(((bf16[2304,512]{1,0:T(8,128)(2,1)}), bf16[1152,512]{1,0:T(8,128)(2,1)}) %reduce-scatter.4.cloned.1.call-update) | async-done | bytes 1179664
  136.3 2.4 copy.91
  141.1 1.5 slice_bitcast_fusion.5
  144.6 5.9 %collective-permute-done.7 = bf16[256,512]{1,0:T(8,128)(2,1)S(1)} collective-permute-done((bf16[256,512]{1,0:T(8,128)(2,1)S(1)}, bf16[256,512]{1,0:T(8,128)(2,1)S(1)}, u32[]{:S(2)}, u32[]{:S(2)}) %collective-permute-start.7) | collective-permute-done | bytes 262176 | tf_op jit(solution)/shard_map/ppermute | solution.py:13
  150.6 1.5 collective-permute-start.8
  154.0 14.2 %collective-permute-done.8 = bf16[256,512]{1,0:T(8,128)(2,1)S(1)} collective-permute-done((bf16[256,512]{1,0:T(8,128)(2,1)S(1)}, bf16[256,512]{1,0:T(8,128)(2,1)S(1)}, u32[]{:S(2)}, u32[]{:S(2)}) %collective-permute-start.8) | collective-permute-done | bytes 262176 | tf_op jit(solution)/shard_map/ppermute | solution.py:13
  169.0 65.9 %all-gather.3.cloned.1.call-done = bf16[9216,512]{0,1:T(8,128)(2,1)} async-done(((bf16[1152,512]{0,1:T(8,128)(2,1)}), bf16[9216,512]{0,1:T(8,128)(2,1)}) %all-gather.3.cloned.1.call-update) | async-done | bytes 9437200 | tf_op jit(solution)/shard_map/all_gather | solution.py:106
  234.9 9.5 %copy.104 = bf16[64,8,8,1152]{3,2,1,0:T(8,128)(2,1)} copy(bf16[64,8,8,1152]{3,1,2,0:T(8,128)(2,1)} %bitcast.177) | data formatting | bytes 18874368
  244.4 11.0 %bitcast_reduce_fusion = bf16[1152,512]{0,1:T(8,128)(2,1)} fusion(bf16[64,8,8,1152]{3,2,1,0:T(8,128)(2,1)} %copy.104), kind=kLoop, calls=%fused_computation.52 | loop fusion | flops 4128768 | bytes 10616832 | tf_op jit(solution)/shard_map/reduce_sum | solution.py:106
  256.9 2.0 copy.85
  (83 shorter events, 24.4 us)
Async XLA Ops:
  7.2 86.3 %copy-start = (bf16[1,256,2304]{2,1,0:T(8,128)(2,1)S(1)}, bf16[1,256,2304]{2,1,0:T(8,128)(2,1)}, u32[]{:S(2)}) copy-start(bf16[1,256,2304]{2,1,0:T(8,128)(2,1)} %param.8) | copy-start | bytes 3538948
  7.2 25.7 %copy-start.7 = (bf16[1,256,1024]{2,1,0:T(8,128)(2,1)S(1)}, bf16[1,256,1024]{2,1,0:T(8,128)(2,1)}, u32[]{:S(2)}) copy-start(bf16[1,256,1024]{2,1,0:T(8,128)(2,1)} %param.12) | copy-start | bytes 1572868
  7.2 129.1 %reduce-scatter.4.cloned.1.call-start = ((), (), s32[]{:S(2)}) async-start(), calls=%async_computation.2 | async-start | bytes 3538944
  8.4 8.1 %collective-permute-start.3 = (bf16[256,512]{0,1:T(8,128)(2,1)S(1)}, bf16[256,512]{0,1:T(8,128)(2,1)S(1)}, u32[]{:S(2)}, u32[]{:S(2)}) collective-permute-start(bf16[256,512]{0,1:T(8,128)(2,1)S(1)} %bitcast.192), channel_id=1, source_target_pairs={{0,1},{1,4},{4,5},{5,8},{8,9},{9,12},{12,13},{2,3},{3,6},{6,7},{7,... | collective-permute-start | bytes 786440 | tf_op jit(solution)/shard_map/ppermute | solution.py:13
  11.9 7.5 %collective-permute-start = (bf16[256,512]{0,1:T(8,128)(2,1)S(1)}, bf16[256,512]{0,1:T(8,128)(2,1)S(1)}, u32[]{:S(2)}, u32[]{:S(2)}) collective-permute-start(bf16[256,512]{0,1:T(8,128)(2,1)S(1)} %bitcast.190), channel_id=1, source_target_pairs={{0,1},{1,4},{4,5},{5,8},{8,9},{9,12},{12,13},{2,3},{3,6},{6,7},{7,... | collective-permute-start | bytes 786440 | tf_op jit(solution)/shard_map/ppermute | solution.py:13
  16.5 7.4 %collective-permute-start.4 = (bf16[256,512]{0,1:T(8,128)(2,1)S(1)}, bf16[256,512]{0,1:T(8,128)(2,1)}, u32[]{:S(2)}, u32[]{:S(2)}) collective-permute-start(bf16[256,512]{0,1:T(8,128)(2,1)S(1)} %collective-permute-done.3), channel_id=1, source_target_pairs={{0,1},{1,4},{4,5},{5,8},{8,9},{9,12},{12,13},{2,3},{3,6},{6,7},{7,... | collective-permute-start | bytes 786440 | tf_op jit(solution)/shard_map/ppermute | solution.py:13
  19.4 8.2 %collective-permute-start.1 = (bf16[256,512]{0,1:T(8,128)(2,1)S(1)}, bf16[256,512]{0,1:T(8,128)(2,1)S(1)}, u32[]{:S(2)}, u32[]{:S(2)}) collective-permute-start(bf16[256,512]{0,1:T(8,128)(2,1)S(1)} %collective-permute-done), channel_id=1, source_target_pairs={{0,1},{1,4},{4,5},{5,8},{8,9},{9,12},{12,13},{2,3},{3,6},{6,7},{7,... | collective-permute-start | bytes 786440 | tf_op jit(solution)/shard_map/ppermute | solution.py:13
  23.9 10.0 %collective-permute-start.5 = (bf16[256,512]{0,1:T(8,128)(2,1)}, bf16[256,512]{0,1:T(8,128)(2,1)}, u32[]{:S(2)}, u32[]{:S(2)}) collective-permute-start(bf16[256,512]{0,1:T(8,128)(2,1)} %collective-permute-done.4), channel_id=1, source_target_pairs={{0,1},{1,4},{4,5},{5,8},{8,9},{9,12},{12,13},{2,3},{3,6},{6,7},{7,... | collective-permute-start | bytes 786440 | tf_op jit(solution)/shard_map/ppermute | solution.py:13
  27.6 8.4 %collective-permute-start.2 = (bf16[256,512]{0,1:T(8,128)(2,1)S(1)}, bf16[256,512]{0,1:T(8,128)(2,1)}, u32[]{:S(2)}, u32[]{:S(2)}) collective-permute-start(bf16[256,512]{0,1:T(8,128)(2,1)S(1)} %collective-permute-done.1), channel_id=1, source_target_pairs={{0,1},{1,4},{4,5},{5,8},{8,9},{9,12},{12,13},{2,3},{3,6},{6,7},{7,... | collective-permute-start | bytes 786440 | tf_op jit(solution)/shard_map/ppermute | solution.py:13
  37.1 5.3 %copy-start.3 = (bf16[1024,2,256]{0,2,1:T(8,128)(2,1)}, bf16[1024,2,256]{0,2,1:T(8,128)(2,1)S(1)}, u32[]{:S(2)}) copy-start(bf16[1024,2,256]{0,2,1:T(8,128)(2,1)S(1)} %get-tuple-element.278) | copy-start | bytes 3145732 | tf_op jit(solution)/shard_map/while
  37.1 5.3 %copy-start.8 = (bf16[256,2,2,256]{0,3,2,1:T(8,128)(2,1)}, bf16[256,2,2,256]{0,3,2,1:T(8,128)(2,1)S(1)}, u32[]{:S(2)}) copy-start(bf16[256,2,2,256]{0,3,2,1:T(8,128)(2,1)S(1)} %get-tuple-element.279) | copy-start | bytes 1572868 | tf_op jit(solution)/shard_map/while
  51.8 3.2 %copy-start.4 = (bf16[1024,2,256]{0,2,1:T(8,128)(2,1)S(1)}, bf16[1024,2,256]{0,2,1:T(8,128)(2,1)}, u32[]{:S(2)}) copy-start(bf16[1024,2,256]{0,2,1:T(8,128)(2,1)} %copy-done.3) | copy-start | bytes 3145732 | tf_op jit(solution)/shard_map/while
  51.8 3.2 %copy-start.9 = (bf16[256,2,2,256]{0,3,2,1:T(8,128)(2,1)S(1)}, bf16[256,2,2,256]{0,3,2,1:T(8,128)(2,1)}, u32[]{:S(2)}) copy-start(bf16[256,2,2,256]{0,3,2,1:T(8,128)(2,1)} %copy-done.8) | copy-start | bytes 1572868 | tf_op jit(solution)/shard_map/while
  55.0 5.3 %copy-start.3 = (bf16[1024,2,256]{0,2,1:T(8,128)(2,1)}, bf16[1024,2,256]{0,2,1:T(8,128)(2,1)S(1)}, u32[]{:S(2)}) copy-start(bf16[1024,2,256]{0,2,1:T(8,128)(2,1)S(1)} %get-tuple-element.278) | copy-start | bytes 3145732 | tf_op jit(solution)/shard_map/while
  55.0 5.3 %copy-start.8 = (bf16[256,2,2,256]{0,3,2,1:T(8,128)(2,1)}, bf16[256,2,2,256]{0,3,2,1:T(8,128)(2,1)S(1)}, u32[]{:S(2)}) copy-start(bf16[256,2,2,256]{0,3,2,1:T(8,128)(2,1)S(1)} %get-tuple-element.279) | copy-start | bytes 1572868 | tf_op jit(solution)/shard_map/while
  69.7 3.2 %copy-start.4 = (bf16[1024,2,256]{0,2,1:T(8,128)(2,1)S(1)}, bf16[1024,2,256]{0,2,1:T(8,128)(2,1)}, u32[]{:S(2)}) copy-start(bf16[1024,2,256]{0,2,1:T(8,128)(2,1)} %copy-done.3) | copy-start | bytes 3145732 | tf_op jit(solution)/shard_map/while
  69.7 3.2 %copy-start.9 = (bf16[256,2,2,256]{0,3,2,1:T(8,128)(2,1)S(1)}, bf16[256,2,2,256]{0,3,2,1:T(8,128)(2,1)}, u32[]{:S(2)}) copy-start(bf16[256,2,2,256]{0,3,2,1:T(8,128)(2,1)} %copy-done.8) | copy-start | bytes 1572868 | tf_op jit(solution)/shard_map/while
  73.9 3.4 %collective-permute-start.9 = (bf16[256,512]{1,0:T(8,128)(2,1)S(1)}, bf16[256,512]{1,0:T(8,128)(2,1)S(1)}, u32[]{:S(2)}, u32[]{:S(2)}) collective-permute-start(bf16[256,512]{1,0:T(8,128)(2,1)S(1)} %bitcast.196), channel_id=1, source_target_pairs={{1,0},{4,1},{5,4},{8,5},{9,8},{12,9},{13,12},{3,2},{6,3},{7,6},{10... | collective-permute-start | bytes 786440 | tf_op jit(solution)/shard_map/ppermute | solution.py:13
  77.5 7.5 %collective-permute-start.10 = (bf16[256,512]{1,0:T(8,128)(2,1)S(1)}, bf16[256,512]{1,0:T(8,128)(2,1)S(1)}, u32[]{:S(2)}, u32[]{:S(2)}) collective-permute-start(bf16[256,512]{1,0:T(8,128)(2,1)S(1)} %add_convert_fusion.2), channel_id=1, source_target_pairs={{1,0},{4,1},{5,4},{8,5},{9,8},{12,9},{13,12},{3,2},{6,3},{7,6},{10... | collective-permute-start | bytes 786440 | tf_op jit(solution)/shard_map/ppermute | solution.py:13
  85.0 7.7 %collective-permute-start.11 = (bf16[256,512]{1,0:T(8,128)(2,1)S(1)}, bf16[256,512]{1,0:T(8,128)(2,1)S(1)}, u32[]{:S(2)}, u32[]{:S(2)}) collective-permute-start(bf16[256,512]{1,0:T(8,128)(2,1)S(1)} %add_convert_fusion.1), channel_id=1, source_target_pairs={{1,0},{4,1},{5,4},{8,5},{9,8},{12,9},{13,12},{3,2},{6,3},{7,6},{10... | collective-permute-start | bytes 786440 | tf_op jit(solution)/shard_map/ppermute | solution.py:13
  86.4 6.3 %copy-start.1 = (f32[2,32,8,256]{3,2,0,1:T(8,128)}, f32[2,32,8,256]{3,2,0,1:T(8,128)S(1)}, u32[]{:S(2)}) copy-start(f32[2,32,8,256]{3,2,0,1:T(8,128)S(1)} %copy.103) | copy-start | bytes 1572868
  92.7 0.7 copy-start.5
  96.7 138.2 %all-gather.3.cloned.1.call-start = ((), (), s32[]{:S(2)}) async-start(), calls=%async_computation.1 | async-start | bytes 10616832 | tf_op jit(solution)/shard_map/all_gather | solution.py:106
  139.8 3.4 %collective-permute-start.6 = (bf16[256,512]{1,0:T(8,128)(2,1)S(1)}, bf16[256,512]{1,0:T(8,128)(2,1)S(1)}, u32[]{:S(2)}, u32[]{:S(2)}) collective-permute-start(bf16[256,512]{1,0:T(8,128)(2,1)S(1)} %bitcast.197), channel_id=1, source_target_pairs={{1,0},{4,1},{5,4},{8,5},{9,8},{12,9},{13,12},{3,2},{6,3},{7,6},{10... | collective-permute-start | bytes 786440 | tf_op jit(solution)/shard_map/ppermute | solution.py:13
  142.5 9.6 %copy-start.10 = (bf16[2,256,2,256]{1,3,2,0:T(8,128)(2,1)S(1)}, bf16[2,256,2,256]{1,3,2,0:T(8,128)(2,1)}, u32[]{:S(2)}) copy-start(bf16[2,256,2,256]{1,3,2,0:T(8,128)(2,1)} %get-tuple-element.58) | copy-start | bytes 1572868
  143.3 7.3 %collective-permute-start.7 = (bf16[256,512]{1,0:T(8,128)(2,1)S(1)}, bf16[256,512]{1,0:T(8,128)(2,1)S(1)}, u32[]{:S(2)}, u32[]{:S(2)}) collective-permute-start(bf16[256,512]{1,0:T(8,128)(2,1)S(1)} %add_convert_fusion.5), channel_id=1, source_target_pairs={{1,0},{4,1},{5,4},{8,5},{9,8},{12,9},{13,12},{3,2},{6,3},{7,6},{10... | collective-permute-start | bytes 786440 | tf_op jit(solution)/shard_map/ppermute | solution.py:13
  144.6 8.6 %copy-start.2 = (f32[2,32,8,256]{3,2,0,1:T(8,128)S(1)}, f32[2,32,8,256]{3,2,0,1:T(8,128)}, u32[]{:S(2)}) copy-start(f32[2,32,8,256]{3,2,0,1:T(8,128)} %copy-done.1) | copy-start | bytes 1572868
  144.6 8.6 %copy-start.6 = (bf16[256,512]{1,0:T(8,128)(2,1)S(1)}, bf16[256,512]{1,0:T(8,128)(2,1)}, u32[]{:S(2)}) copy-start(bf16[256,512]{1,0:T(8,128)(2,1)} %copy-done.5) | copy-start | bytes 786436
  150.6 17.6 %collective-permute-start.8 = (bf16[256,512]{1,0:T(8,128)(2,1)S(1)}, bf16[256,512]{1,0:T(8,128)(2,1)S(1)}, u32[]{:S(2)}, u32[]{:S(2)}) collective-permute-start(bf16[256,512]{1,0:T(8,128)(2,1)S(1)} %add_convert_fusion.4), channel_id=1, source_target_pairs={{1,0},{4,1},{5,4},{8,5},{9,8},{12,9},{13,12},{3,2},{6,3},{7,6},{10... | collective-permute-start | bytes 786440 | tf_op jit(solution)/shard_map/ppermute | solution.py:13
Sparse Core Ops, SparseCore 0:
  96.9 39.3 reduce-scatter.3
  138.8 96.1 all-gather.2
